TPU v7x, 128 devices: a whole 4x4x4 slice. The times are simulated.
128 devices in a mesh: wave: 16 (over y, z_lo, core), pole: 8 (over x, z_hi).
Axes of the slice: x: 4, y: 4, z: 4 (z_hi: 2, z_lo: 2; z = z_hi * 2 + z_lo), core: 2. Of those that a mesh axis runs over, the one named last changes fastest.
Arguments:
- grid: float32 [6, 256, 3072], P(None, None, 'wave'), may hold values from -6 to 6
- legendre: bfloat16 [256, 2, 1536, 1024], P('wave', None, None, 'pole'), may hold values from -0.15625 to 0.15625
- wave_table: int32 [256], replicated, may hold values from 0 to 255, each once
- pole_table: float32 [4, 64], replicated, may hold values from -1.5 to 2.5, as said below
- pole_index: int32 [32], replicated, may hold values from 0 to 63
Outputs:
- next_state: float32 [6, 2, 256, 1024], P(None, None, 'wave', 'pole')
Inputs may be any that keep to these rules, and one draw needn't show every extreme that they name: Slot s holds zonal wavenumber wave_table[s], every wavenumber of 0 to 255 once; row s of legendre belongs to it. `pole_table`: shift real parts lie in 1.5 to 2.5, shift imaginary parts in -1.5 to 1.5, weights in -1.2 to 1.2.
All inputs are finite; a program needn't handle non-finite values.
Results may differ from a plain program's by a relative error of at most 0.0003.
Values sent between devices are 32-bit elements; how exact they have to be, the bound alone decides.
No kernel may reach another device: no remote copies, remote signals or barrier semaphores. Data moves between devices by JAX's collectives and lax.ppermute only.
A program may use at most 128 MiB of HBM per device.

v0:
```python
import jax
import jax.numpy as jnp
from jax import lax
from jax.sharding import PartitionSpec as P

SWEEPS = 8
coriolis_step = 1.2
gravity_step = 0.0008


def split_high(values):
    upper_part = values.astype(jnp.bfloat16)
    kept = lax.optimization_barrier(upper_part)
    lower_part = (values - kept.astype(jnp.float32)).astype(jnp.bfloat16)
    return (upper_part, lower_part)


def coefficients(wavenum, count):
    index = jnp.arange(count, dtype=jnp.int32).astype(jnp.float32)
    parity = jnp.arange(2, dtype=jnp.int32).astype(jnp.float32)
    order = (2.0 * index[None, :] + parity[:, None])[:, None, :]
    wave = wavenum[None, :, None]
    degree = wave + order
    product = degree * (degree + 1.0)
    rossby = coriolis_step * wave / jnp.maximum(product, 2.0)
    gravity = gravity_step * jnp.sqrt(product)
    e_lo = jnp.sqrt(order * (2.0 * wave + order) / jnp.maximum(4.0 * degree * degree - 1.0, 1.0))
    after = order + 1.0
    upper_deg = degree + 1.0
    e_hi = jnp.sqrt(
        after * (2.0 * wave + after) / jnp.maximum(4.0 * upper_deg * upper_deg - 1.0, 1.0)
    )
    return (e_lo, e_hi, rossby, gravity)


def cmul(are, aim, bre, bim):
    return (are * bre - aim * bim, are * bim + aim * bre)


def zero_extend(field):
    return jnp.pad(field, ((0, 0), (0, 0), (0, 0), (0, 0), (1, 1)))


def solve(spectra, coef, shifts, extend):
    e_lo, e_hi, rossby, gravity = coef
    count = spectra.shape[3]
    shift_re = shifts[:, 0][:, None, None, None]
    shift_im = shifts[:, 1][:, None, None, None]
    weight_re = shifts[:, 2][:, None, None, None]
    weight_im = shifts[:, 3][:, None, None, None]
    z0r, z0i = (spectra[0][None], spectra[1][None])
    d0r, d0i = (spectra[2][None], spectra[3][None])
    h0r, h0i = (spectra[4][None], spectra[5][None])
    b_re = shift_re + 0.0 * rossby[None]
    b_im = shift_im + rossby[None]
    b_mag = b_re * b_re + b_im * b_im
    inv_re, inv_im = (b_re / b_mag, -b_im / b_mag)
    det_re, det_im = cmul(b_re, b_im, shift_re, shift_im)
    det_re = det_re + gravity[None] * gravity[None]
    det_mag = det_re * det_re + det_im * det_im
    dinv_re, dinv_im = (det_re / det_mag, -det_im / det_mag)
    grav = gravity[None]
    hb_re, hb_im = cmul(b_re, b_im, h0r, h0i)
    zr, zi, dr, di, hr, hi = (z0r, z0i, d0r, d0i, h0r, h0i)
    for sweep in range(SWEEPS):
        if sweep == 0:
            rzr, rzi, rdr, rdi = (z0r, z0i, d0r, d0i)
        else:
            both = jnp.stack([zr, zi, dr, di], axis=0)
            ext = extend(both)
            lower = jnp.stack([ext[:, :, 1, :, 0:count], ext[:, :, 0, :, 1 : count + 1]], axis=2)
            upper = jnp.stack(
                [ext[:, :, 1, :, 1 : count + 1], ext[:, :, 0, :, 2 : count + 2]], axis=2
            )
            near = e_lo * lower + e_hi * upper
            rzr = z0r - coriolis_step * near[2]
            rzi = z0i - coriolis_step * near[3]
            rdr = d0r + coriolis_step * near[0]
            rdi = d0i + coriolis_step * near[1]
        zr, zi = cmul(rzr, rzi, inv_re, inv_im)
        nd_re, nd_im = cmul(shift_re, shift_im, rdr, rdi)
        nd_re = nd_re + grav * h0r
        nd_im = nd_im + grav * h0i
        nh_re = hb_re - grav * rdr
        nh_im = hb_im - grav * rdi
        dr, di = cmul(nd_re, nd_im, dinv_re, dinv_im)
        hr, hi = cmul(nh_re, nh_im, dinv_re, dinv_im)
    parts = []
    for field_re, field_im in ((zr, zi), (dr, di), (hr, hi)):
        out_re, out_im = cmul(weight_re, weight_im, field_re, field_im)
        parts.append(jnp.sum(out_re, axis=0))
        parts.append(jnp.sum(out_im, axis=0))
    return jnp.stack(parts, axis=0)


def lookup(pole_table, chosen):
    columns = jnp.arange(pole_table.shape[1], dtype=jnp.int32)
    onehot = (chosen[:, None] == columns[None, :]).astype(jnp.float32)
    return jnp.dot(onehot, jnp.transpose(pole_table), precision=lax.Precision.HIGHEST)


def shards(grid, legendre, wave_table, pole_table, pole_index):
    slots = legendre.shape[0]
    local_k = legendre.shape[3]
    lat_rows = grid.shape[2]
    wave_count = lax.axis_size("wave")
    half_count = wave_count // 2
    columns = jnp.take(grid, wave_table, axis=1)
    regrouped = lax.all_to_all(columns[None], "wave", split_axis=2, concat_axis=0, tiled=True)
    north = regrouped[:half_count]
    south = regrouped[half_count:]
    parts = jnp.stack([north + south, north - south], axis=0)
    high, low = split_high(parts)
    leg_blocks = legendre.reshape(slots, 2, half_count, lat_rows, local_k)
    first = jnp.einsum("mpwlk,pwcml->cpmk", leg_blocks, high, preferred_element_type=jnp.float32)
    second = jnp.einsum("mpwlk,pwcml->cpmk", leg_blocks, low, preferred_element_type=jnp.float32)
    spectra = first + second
    own_waves = lax.dynamic_slice_in_dim(wave_table, lax.axis_index("wave") * slots, slots).astype(
        jnp.float32
    )
    whole = lax.all_gather(spectra, "pole", axis=3, tiled=True)
    per_device = pole_index.shape[0] // lax.axis_size("pole")
    chosen = lax.dynamic_slice_in_dim(pole_index, lax.axis_index("pole") * per_device, per_device)
    coef = coefficients(own_waves, whole.shape[3])
    partial_terms = solve(whole, coef, lookup(pole_table, chosen), zero_extend)
    result = lax.psum_scatter(partial_terms, "pole", scatter_dimension=3, tiled=True)
    return result


def solution(mesh):
    in_specs = (P(None, None, "wave"), P("wave", None, None, "pole"), P(), P(), P())
    out_specs = P(None, None, "wave", "pole")
    return jax.shard_map(shards, mesh=mesh, in_specs=in_specs, out_specs=out_specs, check_vma=False)
```

profile of v0, /device:TPU:0, one launch (start us, length us, event | category | flops | bytes accessed | tf_op | source)
XLA Modules:
  0.0 192.9 jit_solution(7145403172599582811)
XLA Ops:
  6.5 0.7 compare_and_fusion
  7.2 0.7 compare_select_fusion
  7.9 2.8 %copy.19 = f32[6,256,192]{2,0,1:T(8,128)} copy(f32[6,256,192]{1,2,0:T(8,128)} %param.5) | data formatting | bytes 2359296 | tf_op args[0]
  10.8 2.3 %gather_fusion = f32[256,6,192]{2,1,0:T(8,128)S(1)} fusion(f32[6,256,192]{2,0,1:T(8,128)} %copy.19, s32[1024]{0:T(1024)S(1)} %pad_clamp_fusion), kind=kCustom, calls=%fused_computation | custom fusion | bytes 2360320 | tf_op jit(solution)/shard_map/jit(_take)/gather | solution.py:108
  13.5 2.8 %copy.20 = f32[1,6,256,192]{3,0,1,2:T(1,128)} copy(f32[1,6,256,192]{3,1,2,0:T(8,128)S(1)} %bitcast_select_fusion) | data formatting | bytes 2359296 | tf_op jit(solution)/shard_map/jit(_take)/select_n | solution.py:108
  16.2 6.1 %all-to-all-start = ((f32[1,6,256,192]{3,0,1,2:T(1,128)}), f32[1,6,256,192]{3,0,1,2:T(1,128)S(1)}, u32[]{:S(2)}, u32[]{:S(2)}) async-start(f32[1,6,256,192]{3,0,1,2:T(1,128)} %copy.20), calls=%async_computation | async-start | bytes 3145728 | tf_op jit(solution)/shard_map/all_to_all | solution.py:109
  23.2 21.3 %all-to-all-done = f32[1,6,256,192]{3,0,1,2:T(1,128)S(1)} async-done(((f32[1,6,256,192]{3,0,1,2:T(1,128)}), f32[1,6,256,192]{3,0,1,2:T(1,128)S(1)}, u32[]{:S(2)}, u32[]{:S(2)}) %all-to-all-start) | async-done | bytes 1179680 | tf_op jit(solution)/shard_map/all_to_all | solution.py:109
  44.7 0.9 copy.56
  46.1 6.8 %fusion.12 = f32[2,16,6,128]{3,2,1,0:T(8,128)S(1)} fusion(bf16[2,8,6,16,192]{4,2,1,3,0:T(8,128)(2,1)S(1)} %fusion.11, bf16[16,2,8,192,128]{4,3,2,1,0:T(8,128)(2,1)} %bitcast.123), kind=kOutput, calls=%fused_computation.72 | convolution fusion | flops 75497472 | bytes 13271040 | tf_op jit(solution)/shard_map/mpwlk,pwcml->cpmk/dot_general | solution.py:115
  53.1 2.2 %fusion.21 = f32[6,2,16,128]{3,0,2,1:T(8,128)S(1)} fusion(f32[2,16,6,128]{3,2,1,0:T(8,128)S(1)} %fusion.12, bf16[16,2,8,192,128]{4,3,2,1,0:T(8,128)(2,1)S(1)} %bitcast.126, bf16[2,8,6,16,192]{4,2,1,3,0:T(8,128)(2,1)S(1)} %fusion.11, f32[1,8,6,16,192]{4,2,1,3,0:T(8,128)S(1)} %get-tuple-element.86, f32[1,8,6,16,192]{4,2,1,3,0:T(8,128)S(1)} %get-tuple-element.85), kind=kOutput, calls=%fused_computation.75 | convolution fusion | flops 76701696 | bytes 14548992 | tf_op jit(solution)/shard_map/mpwlk,pwcml->cpmk/dot_general | solution.py:116
  55.2 37.6 %all_gather.3 = f32[6,2,16,1024]{3,0,2,1:T(8,128)S(1)} all-gather(f32[6,2,16,128]{3,0,2,1:T(8,128)S(1)} %fusion.21), channel_id=1, replica_groups=mesh['wave'=16,'pole'=8] {'pole'}, dimensions={3}, use_global_device_ids=true | all-gather | bytes 884736 | tf_op jit(solution)/shard_map/all_gather | solution.py:121
  92.8 0.9 fusion.99
  93.9 0.8 multiply_subtract_fusion.16
  95.0 0.8 fusion.110
  96.3 0.9 multiply_subtract_fusion.14
  97.4 0.8 fusion.109
  98.8 0.9 multiply_subtract_fusion.12
  99.9 0.8 fusion.108
  101.2 0.9 multiply_subtract_fusion.10
  102.4 0.8 fusion.107
  103.7 0.9 multiply_subtract_fusion.8
  104.8 1.0 fusion.106
  105.9 0.5 fusion.8
  106.4 0.9 multiply_subtract_fusion.6
  107.5 0.8 fusion.105
  108.3 0.5 fusion.9
  108.9 0.9 multiply_subtract_fusion.4
  110.0 0.8 fusion.104
  111.8 0.7 multiply_add_fusion
  112.5 1.1 add_reduce_fusion
  113.7 0.9 copy-done.2
  114.6 71.5 %reduce-scatter.2.cloned.1.call-done = f32[6,2,16,128]{3,2,1,0:T(8,128)} async-done(((f32[6,2,16,1024]{3,2,1,0:T(8,128)}), f32[6,2,16,128]{3,2,1,0:T(8,128)}) %reduce-scatter.2.cloned.1.call-update) | async-done | bytes 98320 | tf_op jit(solution)/shard_map/reduce_scatter | solution.py:126
  (55 shorter events, 6.4 us)
Async XLA Ops:
  6.5 16.1 %copy-start = (f32[4,64]{1,0:T(4,128)S(1)}, f32[4,64]{1,0:T(4,128)}, u32[]{:S(2)}) copy-start(f32[4,64]{1,0:T(4,128)} %param.8) | copy-start | bytes 3076
  16.2 6.2 %copy-start.3 = (s32[256]{0:T(256)S(1)}, s32[256]{0:T(256)}, u32[]{:S(2)}) copy-start(s32[256]{0:T(256)} %param.7) | copy-start | bytes 3076
  16.2 6.3 %copy-start.4 = (s32[32]{0:T(128)S(1)}, s32[32]{0:T(128)}, u32[]{:S(2)}) copy-start(s32[32]{0:T(128)} %param.9) | copy-start | bytes 388
  16.2 28.2 %all-to-all-start = ((f32[1,6,256,192]{3,0,1,2:T(1,128)}), f32[1,6,256,192]{3,0,1,2:T(1,128)S(1)}, u32[]{:S(2)}, u32[]{:S(2)}) async-start(f32[1,6,256,192]{3,0,1,2:T(1,128)} %copy.20), calls=%async_computation | async-start | bytes 3145728 | tf_op jit(solution)/shard_map/all_to_all | solution.py:109
  22.4 163.6 %reduce-scatter.2.cloned.1.call-start = ((), (), s32[]{:S(2)}) async-start(), calls=%async_computation.2 | async-start | bytes 884736 | tf_op jit(solution)/shard_map/reduce_scatter | solution.py:126
  44.6 8.3 %slice-start = ((s8[12582912]{0:T(1024)(128)(4,1)}), s8[4194304]{0:T(1024)(128)(4,1)S(1)}, s32[]{:S(2)}) async-start(s8[12582912]{0:T(1024)(128)(4,1)} %bitcast.124), calls=%async_computation.3 | async-start | bytes 8388608
  45.8 7.1 %slice-start.1 = ((s8[12582912]{0:T(1024)(128)(4,1)}), s8[4194304]{0:T(1024)(128)(4,1)S(1)}, s32[]{:S(2)}) async-start(s8[12582912]{0:T(1024)(128)(4,1)} %bitcast.124), calls=%async_computation.4 | async-start | bytes 8388608
  46.1 6.9 %slice-start.2 = ((s8[12582912]{0:T(1024)(128)(4,1)}), s8[4194304]{0:T(1024)(128)(4,1)S(1)}, s32[]{:S(2)}) async-start(s8[12582912]{0:T(1024)(128)(4,1)} %bitcast.124), calls=%async_computation.5 | async-start | bytes 8388608
  112.5 73.6 %copy-start.1 = (f32[4,64]{1,0:T(4,128)S(1)}, f32[4,64]{1,0:T(4,128)}, u32[]{:S(2)}) copy-start(f32[4,64]{1,0:T(4,128)} %param.8) | copy-start | bytes 3076
  113.7 0.9 copy-start.2
Sparse Core Ops, SparseCore 0:
  114.7 71.3 reduce-scatter.1
where the time goes:
time: 193 us
  waiting for transfers between devices  92.8 us (48%)
  blocking collectives  37.6 us (19%)
  other arithmetic  17 us (9%)
  local copies, waits for them, and re-layouts  16.4 us (8%)
  between operations  13.8 us (7%)
  matrix products  9.14 us (5%)
  starting transfers between devices  6.18 us (3%)
    reduce_scatter x1, waiting for transfers between devices, shards(): lax.psum_scatter(partial_terms, 'pole', scatter_dimension=3, tiled=True)  71.5 us
    all_gather x1, blocking collectives, shards(): whole = lax.all_gather(spectra, 'pole', axis=3, tiled=True)  37.6 us
    all_to_all x1, waiting for transfers between devices, shards(): lax.all_to_all(columns[None], 'wave', split_axis=2, concat_axis=0, tiled=...  21.3 us
    dot_general x1, matrix products, shards(): jnp.einsum('mpwlk,pwcml->cpmk', leg_blocks, high, preferred_element_type=...  6.8 us
    sub x8, other arithmetic, cmul(): return (are * bre - aim * bim, are * bim + aim * bre)  6.75 us
    all_to_all x1, starting transfers between devices, shards(): lax.all_to_all(columns[None], 'wave', split_axis=2, concat_axis=0, tiled=...  6.14 us
    slice x7, local copies, waits for them, and re-layouts, solve(): ext[:, :, 1, :, 1:count + 1]  5.96 us
    unnamed x26, local copies, waits for them, and re-layouts  4.13 us
  transfers between devices with their start and end apart: 2, of which 2 were waited for; matrix products, arithmetic and copies ran while one was open for 0% of the time, Pallas kernels for 0%

commit v1 on v0

--- a/solution.py
+++ b/solution.py
@@ -106,7 +106,12 @@
     wave_count = lax.axis_size("wave")
     half_count = wave_count // 2
     columns = jnp.take(grid, wave_table, axis=1)
-    regrouped = lax.all_to_all(columns[None], "wave", split_axis=2, concat_axis=0, tiled=True)
+    regrouped = jnp.concatenate(
+        lax.all_to_all(
+            jnp.stack(jnp.split(columns[None], lax.axis_size("wave"), axis=2)), "wave", 0, 0
+        ),
+        axis=0,
+    )
     north = regrouped[:half_count]
     south = regrouped[half_count:]
     parts = jnp.stack([north + south, north - south], axis=0)

time: 193 us -> 192 us (level)
    select_n x1 -> x0, local copies, waits for them, and re-layouts: 2.78 us -> none  [shards(): columns = jnp.take(grid, wave_table, axis=1)]
    unnamed x26 -> x41, local copies, waits for them, and re-layouts: 4.13 us -> 4.33 us
where the time goes in v1:
time: 192 us
  waiting for transfers between devices  92.8 us (48%)
  blocking collectives  37.6 us (20%)
  other arithmetic  17.7 us (9%)
  local copies, waits for them, and re-layouts  14.5 us (8%)
  between operations  13.9 us (7%)
  matrix products  9.3 us (5%)
  starting transfers between devices  6.18 us (3%)
    reduce_scatter x1, waiting for transfers between devices, shards(): lax.psum_scatter(partial_terms, 'pole', scatter_dimension=3, tiled=True)  71.5 us
    all_gather x1, blocking collectives, shards(): whole = lax.all_gather(spectra, 'pole', axis=3, tiled=True)  37.6 us
    all_to_all x1, waiting for transfers between devices, shards(): lax.all_to_all(jnp.stack(jnp.split(columns[None], lax.axis_size('wave'),...  21.3 us
    dot_general x1, matrix products, shards(): jnp.einsum('mpwlk,pwcml->cpmk', leg_blocks, high, preferred_element_type=...  6.97 us
    sub x8, other arithmetic, cmul(): return (are * bre - aim * bim, are * bim + aim * bre)  6.75 us
    all_to_all x1, starting transfers between devices, shards(): lax.all_to_all(jnp.stack(jnp.split(columns[None], lax.axis_size('wave'),...  6.14 us
    slice x7, local copies, waits for them, and re-layouts, solve(): ext[:, :, 1, :, 1:count + 1]  5.96 us
    unnamed x41, local copies, waits for them, and re-layouts  4.33 us
  transfers between devices with their start and end apart: 2, of which 2 were waited for; matrix products, arithmetic and copies ran while one was open for 0% of the time, Pallas kernels for 0%

profile of v1, /device:TPU:0, one launch (start us, length us, event | category | flops | bytes accessed | tf_op | source)
XLA Modules:
  0.0 192.0 jit_solution(8708339376040782265)
XLA Ops:
  6.5 0.7 compare_and_fusion
  7.2 0.7 compare_select_fusion
  7.9 2.8 %copy.47 = f32[6,256,192]{2,0,1:T(8,128)} copy(f32[6,256,192]{1,2,0:T(8,128)} %param.5) | data formatting | bytes 2359296 | tf_op args[0]
  10.8 2.3 %gather_fusion = f32[256,6,192]{2,1,0:T(8,128)S(1)} fusion(f32[6,256,192]{2,0,1:T(8,128)} %copy.47, s32[1024]{0:T(1024)S(1)} %pad_clamp_fusion), kind=kCustom, calls=%fused_computation | custom fusion | bytes 2360320 | tf_op jit(solution)/shard_map/jit(_take)/gather | solution.py:108
  13.8 1.7 copy.48
  15.4 6.1 %all-to-all-start = ((f32[16,1,6,16,192]{4,3,2,1,0:T(8,128)}), f32[16,1,6,16,192]{4,3,2,1,0:T(8,128)S(1)}, u32[]{:S(2)}, u32[]{:S(2)}) async-start(f32[16,1,6,16,192]{4,3,2,1,0:T(8,128)} %copy.48), calls=%async_computation | async-start | bytes 3145728 | tf_op jit(solution)/shard_map/all_to_all | solution.py:110
  22.4 21.3 %all-to-all-done = f32[16,1,6,16,192]{4,3,2,1,0:T(8,128)S(1)} async-done(((f32[16,1,6,16,192]{4,3,2,1,0:T(8,128)}), f32[16,1,6,16,192]{4,3,2,1,0:T(8,128)S(1)}, u32[]{:S(2)}, u32[]{:S(2)}) %all-to-all-start) | async-done | bytes 1179680 | tf_op jit(solution)/shard_map/all_to_all | solution.py:110
  43.8 0.9 fusion.24
  45.0 7.0 %fusion.12 = f32[2,16,6,128]{3,2,1,0:T(8,128)S(1)} fusion(bf16[2,8,6,16,192]{4,2,1,3,0:T(8,128)(2,1)S(1)} %fusion.11, bf16[16,2,8,192,128]{4,3,2,1,0:T(8,128)(2,1)} %bitcast.183), kind=kOutput, calls=%fused_computation.71 | convolution fusion | flops 75497472 | bytes 13271040 | tf_op jit(solution)/shard_map/mpwlk,pwcml->cpmk/dot_general | solution.py:120
  52.1 2.2 %fusion.21 = f32[6,2,16,128]{3,0,2,1:T(8,128)S(1)} fusion(f32[2,16,6,128]{3,2,1,0:T(8,128)S(1)} %fusion.12, bf16[16,2,8,192,128]{4,3,2,1,0:T(8,128)(2,1)S(1)} %bitcast.186, bf16[2,8,6,16,192]{4,2,1,3,0:T(8,128)(2,1)S(1)} %fusion.11, f32[1,8,6,16,192]{4,2,1,3,0:T(8,128)S(1)} %get-tuple-element.86, f32[1,8,6,16,192]{4,2,1,3,0:T(8,128)S(1)} %get-tuple-element.85), kind=kOutput, calls=%fused_computation.74 | convolution fusion | flops 76701696 | bytes 14548992 | tf_op jit(solution)/shard_map/mpwlk,pwcml->cpmk/dot_general | solution.py:121
  54.3 37.6 %all_gather.3 = f32[6,2,16,1024]{3,0,2,1:T(8,128)S(1)} all-gather(f32[6,2,16,128]{3,0,2,1:T(8,128)S(1)} %fusion.21), channel_id=1, replica_groups=mesh['wave'=16,'pole'=8] {'pole'}, dimensions={3}, use_global_device_ids=true | all-gather | bytes 884736 | tf_op jit(solution)/shard_map/all_gather | solution.py:126
  91.8 0.9 fusion.117
  93.0 0.8 multiply_subtract_fusion.16
  94.0 0.8 fusion.128
  95.4 0.9 multiply_subtract_fusion.14
  96.5 0.8 fusion.127
  97.9 0.9 multiply_subtract_fusion.12
  99.0 0.8 fusion.126
  100.4 0.9 multiply_subtract_fusion.10
  101.5 0.8 fusion.125
  102.8 0.9 multiply_subtract_fusion.8
  104.0 1.0 fusion.124
  105.0 0.5 fusion.8
  105.5 0.9 multiply_subtract_fusion.6
  106.6 0.8 fusion.123
  107.5 0.5 fusion.9
  108.0 0.9 multiply_subtract_fusion.4
  109.1 0.8 fusion.122
  110.9 0.7 multiply_add_fusion
  111.6 1.1 add_reduce_fusion
  112.8 0.9 copy-done.2
  113.7 71.5 %reduce-scatter.2.cloned.1.call-done = f32[6,2,16,128]{3,2,1,0:T(8,128)} async-done(((f32[6,2,16,1024]{3,2,1,0:T(8,128)}), f32[6,2,16,128]{3,2,1,0:T(8,128)}) %reduce-scatter.2.cloned.1.call-update) | async-done | bytes 98320 | tf_op jit(solution)/shard_map/reduce_scatter | solution.py:131
  (70 shorter events, 6.5 us)
Async XLA Ops:
  6.5 15.3 %copy-start = (f32[4,64]{1,0:T(4,128)S(1)}, f32[4,64]{1,0:T(4,128)}, u32[]{:S(2)}) copy-start(f32[4,64]{1,0:T(4,128)} %param.8) | copy-start | bytes 3076
  15.4 6.2 %copy-start.3 = (s32[256]{0:T(256)S(1)}, s32[256]{0:T(256)}, u32[]{:S(2)}) copy-start(s32[256]{0:T(256)} %param.7) | copy-start | bytes 3076
  15.4 6.3 %copy-start.4 = (s32[32]{0:T(128)S(1)}, s32[32]{0:T(128)}, u32[]{:S(2)}) copy-start(s32[32]{0:T(128)} %param.9) | copy-start | bytes 388
  15.4 28.2 %all-to-all-start = ((f32[16,1,6,16,192]{4,3,2,1,0:T(8,128)}), f32[16,1,6,16,192]{4,3,2,1,0:T(8,128)S(1)}, u32[]{:S(2)}, u32[]{:S(2)}) async-start(f32[16,1,6,16,192]{4,3,2,1,0:T(8,128)} %copy.48), calls=%async_computation | async-start | bytes 3145728 | tf_op jit(solution)/shard_map/all_to_all | solution.py:110
  21.6 163.6 %reduce-scatter.2.cloned.1.call-start = ((), (), s32[]{:S(2)}) async-start(), calls=%async_computation.2 | async-start | bytes 884736 | tf_op jit(solution)/shard_map/reduce_scatter | solution.py:131
  43.7 8.3 %slice-start = ((s8[12582912]{0:T(1024)(128)(4,1)}), s8[4194304]{0:T(1024)(128)(4,1)S(1)}, s32[]{:S(2)}) async-start(s8[12582912]{0:T(1024)(128)(4,1)} %bitcast.184), calls=%async_computation.3 | async-start | bytes 8388608
  44.7 7.3 %slice-start.1 = ((s8[12582912]{0:T(1024)(128)(4,1)}), s8[4194304]{0:T(1024)(128)(4,1)S(1)}, s32[]{:S(2)}) async-start(s8[12582912]{0:T(1024)(128)(4,1)} %bitcast.184), calls=%async_computation.4 | async-start | bytes 8388608
  45.0 7.1 %slice-start.2 = ((s8[12582912]{0:T(1024)(128)(4,1)}), s8[4194304]{0:T(1024)(128)(4,1)S(1)}, s32[]{:S(2)}) async-start(s8[12582912]{0:T(1024)(128)(4,1)} %bitcast.184), calls=%async_computation.5 | async-start | bytes 8388608
  111.6 73.6 %copy-start.1 = (f32[4,64]{1,0:T(4,128)S(1)}, f32[4,64]{1,0:T(4,128)}, u32[]{:S(2)}) copy-start(f32[4,64]{1,0:T(4,128)} %param.8) | copy-start | bytes 3076
  112.8 0.9 copy-start.2
Sparse Core Ops, SparseCore 0:
  113.8 71.3 reduce-scatter.1
